TPU v7x, 256 devices: a whole 4x4x8 slice. The times are simulated.
256 devices in a mesh: ctx: 16 (over z, core), ch: 16 (over y, x).
Axes of the slice: x: 4, y: 4, z: 8, core: 2. Of those that a mesh axis runs over, the one named last changes fastest.
Arguments:
- inputs: bfloat16 [4096, 4096], P('ctx', 'ch'), may hold values from -6 to 6
- gating: bfloat16 [4096, 4096], P('ctx', 'ch'), may hold values from -6 to 6
- filter_taps: bfloat16 [4096, 4096], P('ctx', 'ch'), may hold values from -2.25 to 2.25
- skip_gain: float32 [4096], P('ch'), may hold values from 0.5 to 1.5
- w_out: bfloat16 [4096, 4096], P('ch'), may hold values from -0.09375 to 0.09375
- cotangent: bfloat16 [4096, 4096], P('ctx', 'ch'), may hold values from -0.3125 to 0.3125
Outputs:
- output: bfloat16 [4096, 4096], P('ctx', 'ch')
- filter_grad: float32 [4096, 4096], P('ctx', 'ch')
All inputs are finite; a program needn't handle non-finite values.
Results may differ from a plain program's by a relative error of at most 0.015.
Values may be sent and summed in bfloat16 or wider, within the bound.
No kernel may reach another device: no remote copies, remote signals or barrier semaphores. Data moves between devices by JAX's collectives and lax.ppermute only.
A program may use at most 64 MiB of HBM per device.

v0:
```python
import math
import jax
import jax.numpy as jnp
from jax import lax
from jax.sharding import PartitionSpec as P

exact_prec = lax.Precision.HIGHEST


def spectral_tables(block_len):
    time_ids = jnp.arange(2 * block_len, dtype=jnp.int32)
    freq_ids = jnp.arange(block_len, dtype=jnp.int32)
    phase_ids = freq_ids[:, None] * time_ids[None, :] % (2 * block_len)
    angles = phase_ids.astype(jnp.float32) * (math.pi / block_len)
    parity = jnp.where(time_ids % 2 == 0, 1.0, -1.0).astype(jnp.float32)[None, :]
    is_first = (freq_ids == 0)[:, None]
    forward = jnp.concatenate(
        [jnp.cos(angles), jnp.where(is_first, parity, -jnp.sin(angles))], axis=0
    )
    norm_scale = 1.0 / (2 * block_len)
    real_rows = jnp.where(is_first, 1.0, 2.0) * jnp.cos(angles) * norm_scale
    imag_rows = jnp.where(is_first, parity, -2.0 * jnp.sin(angles)) * norm_scale
    inverse = jnp.concatenate([real_rows, imag_rows], axis=0).T
    first_bin = is_first.astype(jnp.float32)
    return (forward, inverse, first_bin)


def spec_product(first_spec, second_spec, first_bin):
    bin_count = first_bin.shape[0]
    first_real, first_imag = (first_spec[..., :bin_count, :], first_spec[..., bin_count:, :])
    second_real, second_imag = (second_spec[..., :bin_count, :], second_spec[..., bin_count:, :])
    others = 1.0 - first_bin
    real_part = first_real * second_real - others * first_imag * second_imag
    imag_part = (
        others * (first_real * second_imag + first_imag * second_real)
        + first_bin * first_imag * second_imag
    )
    return jnp.concatenate([real_part, imag_part], axis=-2)


def conj_product(first_spec, second_spec, first_bin):
    bin_count = first_bin.shape[0]
    first_real, first_imag = (first_spec[..., :bin_count, :], first_spec[..., bin_count:, :])
    second_real, second_imag = (second_spec[..., :bin_count, :], second_spec[..., bin_count:, :])
    others = 1.0 - first_bin
    real_part = first_real * second_real + others * first_imag * second_imag
    imag_part = (
        others * (first_imag * second_real - first_real * second_imag)
        + first_bin * first_imag * second_imag
    )
    return jnp.concatenate([real_part, imag_part], axis=-2)


def transform(dft_table, block_rows):
    return jnp.dot(dft_table, block_rows.astype(jnp.float32), precision=exact_prec)


def shift_blocks(spec, blocks, width):
    if blocks == 0:
        return spec
    rows = spec.shape[0]
    pad = jnp.zeros((rows, blocks * width), spec.dtype)
    return jnp.concatenate([pad, spec[:, : spec.shape[1] - blocks * width]], axis=1)


def body(inputs, gating, filter_taps, skip_gain, w_out, cotangent):
    block_len, channels = inputs.shape
    ctx_count = lax.axis_size("ctx")
    width = channels // ctx_count
    forward, inverse, first_bin = spectral_tables(block_len)
    first_half = forward[:, :block_len]
    second_half = forward[:, block_len:]
    pair = jnp.stack([inputs, filter_taps])
    pair_t = lax.all_to_all(pair, "ctx", 2, 2, tiled=True)
    signal_t, taps_t = (pair_t[0], pair_t[1])
    upstream = lax.dot_general(
        lax.all_gather(cotangent, "ch", axis=1, tiled=True),
        w_out,
        (((1,), (1,)), ((), ())),
        preferred_element_type=jnp.float32,
    )
    gate_wide = gating.astype(jnp.float32)
    grad_mixed = upstream * gate_wide
    grad_t = lax.all_to_all(grad_mixed, "ctx", 1, 1, tiled=True)
    low_spec = transform(first_half, signal_t)
    high_spec = transform(second_half, signal_t)
    seg_spec = high_spec + shift_blocks(low_spec, 1, width)
    taps_spec = transform(first_half, taps_t)
    grad_spec = transform(second_half, grad_t)
    running = jnp.zeros_like(seg_spec)
    lag_terms = []
    for lag in range(ctx_count):
        shifted = shift_blocks(seg_spec, lag, width)
        tap_block = taps_spec[:, lag * width : (lag + 1) * width]
        running = running + spec_product(jnp.tile(tap_block, (1, ctx_count)), shifted, first_bin)
        term = conj_product(grad_spec, shifted, first_bin)
        lag_terms.append(term.reshape(term.shape[0], ctx_count, width).sum(axis=1))
    lag_spec = jnp.concatenate(lag_terms, axis=1)
    convolved_t = jnp.dot(inverse[block_len:], running, precision=exact_prec)
    filter_grad_t = jnp.dot(inverse[:block_len], lag_spec, precision=exact_prec)
    back = lax.all_to_all(jnp.stack([convolved_t, filter_grad_t]), "ctx", 2, 2, tiled=True)
    convolved, filter_grad = (back[0], back[1])
    mixed_sum = convolved + skip_gain[None, :] * inputs.astype(jnp.float32)
    gated_rows = (gate_wide * mixed_sum).astype(jnp.bfloat16)
    partial_out = jnp.dot(gated_rows, w_out, preferred_element_type=jnp.float32)
    output = lax.psum_scatter(
        partial_out.astype(jnp.bfloat16), "ch", scatter_dimension=1, tiled=True
    )
    return (output, filter_grad)


def solution(mesh):
    return jax.shard_map(
        body,
        mesh=mesh,
        in_specs=(
            P("ctx", "ch"),
            P("ctx", "ch"),
            P("ctx", "ch"),
            P("ch"),
            P("ch", None),
            P("ctx", "ch"),
        ),
        out_specs=(P("ctx", "ch"), P("ctx", "ch")),
        check_vma=False,
    )
```

profile of v0, /device:TPU:2, one launch (start us, length us, event | category | flops | bytes accessed | tf_op | source)
XLA Modules:
  0.0 263.9 jit_solution(2376567963497250367)
XLA Ops:
  9.8 8.6 %all-to-all-start = ((bf16[2,256,256]{1,0,2:T(2,128)(2,1)}), bf16[2,256,256]{1,0,2:T(2,128)(2,1)S(1)}, u32[]{:S(2)}, u32[]{:S(2)}) async-start(bf16[2,256,256]{1,0,2:T(2,128)(2,1)} %copy.25), calls=%async_computation | async-start | bytes 524288 | tf_op jit(solution)/shard_map/all_to_all | solution.py:74
  19.4 1.9 fusion.170
  21.3 2.0 multiply_multiply_fusion
  23.3 2.0 select_multiply_fusion
  26.5 3.0 %all-to-all-done = bf16[2,256,256]{1,0,2:T(2,128)(2,1)S(1)} async-done(((bf16[2,256,256]{1,0,2:T(2,128)(2,1)}), bf16[2,256,256]{1,0,2:T(2,128)(2,1)S(1)}, u32[]{:S(2)}, u32[]{:S(2)}) %all-to-all-start) | async-done | bytes 262176 | tf_op jit(solution)/shard_map/all_to_all | solution.py:74
  29.5 1.2 fusion.195
  32.8 1.3 fusion.173
  34.1 1.3 fusion.175
  35.3 29.8 %all-gather.2.cloned.1.call-done = bf16[256,4096]{1,0:T(8,128)(2,1)} async-done(((bf16[256,256]{1,0:T(8,128)(2,1)}), bf16[256,4096]{1,0:T(8,128)(2,1)}) %all-gather.2.cloned.1.call-update) | async-done | bytes 2097168 | tf_op jit(solution)/shard_map/all_gather | solution.py:77
  65.1 3.0 %convolution_multiply_fusion = f32[256,256]{0,1:T(8,128)} fusion(bf16[256,4096]{1,0:T(8,128)(2,1)} %all-gather.2.cloned.1.call-done, bf16[256,4096]{1,0:T(8,128)(2,1)S(1)} %copy-done, bf16[256,256]{0,1:T(8,128)(2,1)S(1)} %copy.24), kind=kOutput, calls=%fused_computation.4 | convolution fusion | flops 537001984 | bytes 4587520 | tf_op jit(solution)/shard_map/dot_general | solution.py:76
  68.1 7.1 %all-to-all-start.1 = ((f32[256,16,16]{0,2,1:T(8,128)}), f32[256,16,16]{0,2,1:T(8,128)S(1)}, u32[]{:S(2)}, u32[]{:S(2)}) async-start(f32[256,16,16]{0,2,1:T(8,128)} %bitcast.38), calls=%async_computation.1 | async-start | bytes 524288 | tf_op jit(solution)/shard_map/all_to_all | solution.py:84
  75.3 1.6 convolution_add_fusion
  80.2 1.3 fusion.128
  82.2 4.2 %all-to-all-done.1 = f32[256,16,16]{0,2,1:T(8,128)S(1)} async-done(((f32[256,16,16]{0,2,1:T(8,128)}), f32[256,16,16]{0,2,1:T(8,128)S(1)}, u32[]{:S(2)}, u32[]{:S(2)}) %all-to-all-start.1) | async-done | bytes 262176 | tf_op jit(solution)/shard_map/all_to_all | solution.py:84
  86.4 1.7 fusion.171
  88.1 1.7 fusion.72
  90.5 2.7 %fusion.76 = (f32[256,256]{0,1:T(8,128)}, f32[256,256]{0,1:T(8,128)}, f32[256,256]{0,1:T(8,128)S(1)}, f32[256,256]{0,1:T(8,128)S(1)}, f32[256,256]{0,1:T(8,128)S(1)}, /*index=5*/f32[256,256]{0,1:T(8,128)S(1)}) fusion(f32[256,16]{0,1:T(8,128)S(1)} %copy-done.40, f32[256,16]{0,1:T(8,128)S(1)} %copy-done.41, f32[256]{0:T(256)S(1)} %broadcast_subtract_fusion, ...), kind=kLoop, calls=%fused_computation.219 | loop fusion | flops 2031616 | bytes 2656256 | tf_op jit(solution)/shard_map/sub | solution.py:33
  94.4 1.7 reduce_sum.145
  96.1 1.7 reduce_sum.159
  99.7 1.7 reduce_sum.147
  102.0 2.0 fusion.88
  105.2 1.7 reduce_sum.148
  110.0 1.7 reduce_sum.146
  112.3 2.1 fusion.92
  115.4 1.7 reduce_sum.149
  117.7 1.9 fusion.132
  120.5 1.7 reduce_sum.152
  124.1 1.7 reduce_sum.151
  126.4 2.1 fusion.96
  129.6 1.7 reduce_sum.150
  131.3 1.7 reduce_sum.154
  133.7 1.4 constant_dynamic-update-slice_fusion.13
  135.1 1.4 constant_dynamic-update-slice_fusion.12
  136.4 1.4 constant_dynamic-update-slice_fusion.11
  137.8 1.4 constant_dynamic-update-slice_fusion.10
  139.1 1.4 constant_dynamic-update-slice_fusion.9
  140.5 1.4 constant_dynamic-update-slice_fusion.8
  141.9 1.4 constant_dynamic-update-slice_fusion.7
  143.2 1.4 constant_dynamic-update-slice_fusion.6
  144.6 1.4 constant_dynamic-update-slice_fusion.5
  145.9 1.4 constant_dynamic-update-slice_fusion.4
  148.5 1.4 constant_dynamic-update-slice_fusion.1
  150.5 2.0 convolution_bitcast_fusion
  152.6 4.2 %convolution_bitcast_fusion.1 = f32[1,256,256]{2,1,0:T(8,128)S(1)} fusion(f32[512,512]{0,1:T(8,128)S(1)} %copy-done.4, f32[256,256]{0,1:T(8,128)} %get-tuple-element.37, f32[256,256]{0,1:T(8,128)S(1)} %copy-done.21, f32[256,256]{0,1:T(8,128)} %get-tuple-element.57, f32[256,256]{0,1:T(8,128)} %get-tuple-element.56, f32[256,256]{0,1:T(8,128)} %get-tuple-element.97, ...), kind=kOutput, calls=%fused_computation.3 | convolution fusion | flops 406716416 | bytes 9175040 | tf_op jit(solution)/shard_map/dot_general | solution.py:99
  157.9 3.6 %all-to-all-start.2 = ((f32[2,256,256]{1,0,2:T(2,128)}), f32[2,256,256]{1,0,2:T(2,128)S(1)}, u32[]{:S(2)}, u32[]{:S(2)}) async-start(f32[2,256,256]{1,0,2:T(2,128)} %copy.30), calls=%async_computation.2 | async-start | bytes 1048576 | tf_op jit(solution)/shard_map/all_to_all | solution.py:101
  161.6 15.8 %all-to-all-done.2 = f32[2,256,256]{1,0,2:T(2,128)S(1)} async-done(((f32[2,256,256]{1,0,2:T(2,128)}), f32[2,256,256]{1,0,2:T(2,128)S(1)}, u32[]{:S(2)}, u32[]{:S(2)}) %all-to-all-start.2) | async-done | bytes 524320 | tf_op jit(solution)/shard_map/all_to_all | solution.py:101
  177.9 2.2 convolution_convert_fusion
  180.9 76.1 %reduce-scatter.2.cloned.1.call-done = bf16[256,256]{1,0:T(8,128)(2,1)} async-done(((bf16[256,4096]{1,0:T(8,128)(2,1)}), bf16[256,256]{1,0:T(8,128)(2,1)}) %reduce-scatter.2.cloned.1.call-update) | async-done | bytes 131088 | tf_op jit(solution)/shard_map/reduce_scatter | solution.py:106
  (154 shorter events, 31.2 us)
Async XLA Ops:
  7.2 57.9 %copy-start = (bf16[256,4096]{1,0:T(8,128)(2,1)S(1)}, bf16[256,4096]{1,0:T(8,128)(2,1)}, u32[]{:S(2)}) copy-start(bf16[256,4096]{1,0:T(8,128)(2,1)} %param.10) | copy-start | bytes 6291460
  7.2 57.9 %all-gather.2.cloned.1.call-start = ((), (), s32[]{:S(2)}) async-start(), calls=%async_computation.4 | async-start | bytes 2228224 | tf_op jit(solution)/shard_map/all_gather | solution.py:77
  9.8 19.7 %all-to-all-start = ((bf16[2,256,256]{1,0,2:T(2,128)(2,1)}), bf16[2,256,256]{1,0,2:T(2,128)(2,1)S(1)}, u32[]{:S(2)}, u32[]{:S(2)}) async-start(bf16[2,256,256]{1,0,2:T(2,128)(2,1)} %copy.25), calls=%async_computation | async-start | bytes 524288 | tf_op jit(solution)/shard_map/all_to_all | solution.py:74
  19.4 45.7 %copy-start.10 = (bf16[256,256]{0,1:T(8,128)(2,1)}, bf16[256,256]{0,1:T(8,128)(2,1)S(1)}, u32[]{:S(2)}) copy-start(bf16[256,256]{0,1:T(8,128)(2,1)S(1)} %copy.24) | copy-start | bytes 393220
  21.3 53.9 %copy-start.2 = (f32[256,512]{1,0:T(8,128)}, f32[256,512]{1,0:T(8,128)S(1)}, u32[]{:S(2)}) copy-start(f32[256,512]{1,0:T(8,128)S(1)} %fusion.170) | copy-start | bytes 1572868
  25.4 8.7 %copy-start.3 = (f32[256,512]{1,0:T(8,128)}, f32[256,512]{1,0:T(8,128)S(1)}, u32[]{:S(2)}) copy-start(f32[256,512]{1,0:T(8,128)S(1)} %get-tuple-element.153) | copy-start | bytes 1572868
  68.1 18.3 %all-to-all-start.1 = ((f32[256,16,16]{0,2,1:T(8,128)}), f32[256,16,16]{0,2,1:T(8,128)S(1)}, u32[]{:S(2)}, u32[]{:S(2)}) async-start(f32[256,16,16]{0,2,1:T(8,128)} %bitcast.38), calls=%async_computation.1 | async-start | bytes 524288 | tf_op jit(solution)/shard_map/all_to_all | solution.py:84
  76.8 11.2 %copy-start.1 = (f32[512,256]{0,1:T(8,128)}, f32[512,256]{0,1:T(8,128)S(1)}, u32[]{:S(2)}) copy-start(f32[512,256]{0,1:T(8,128)S(1)} %convolution_add_fusion) | copy-start | bytes 1572868
  76.9 13.7 %copy-start.25 = (f32[512,16]{0,1:T(8,128)}, f32[512,16]{0,1:T(8,128)S(1)}, u32[]{:S(2)}) copy-start(f32[512,16]{0,1:T(8,128)S(1)} %slice.604) | copy-start | bytes 98308
  76.9 3.3 %copy-start.22 = (f32[512,32]{0,1:T(8,128)}, f32[512,32]{0,1:T(8,128)S(1)}, u32[]{:S(2)}) copy-start(f32[512,32]{0,1:T(8,128)S(1)} %slice.601) | copy-start | bytes 196612
  93.2 4.5 %slice-start.5 = ((f32[512,256]{0,1:T(8,128)}), f32[512,208]{0,1:T(8,128)S(1)}, s32[]{:S(2)}) async-start(f32[512,256]{0,1:T(8,128)} %copy-done.1), calls=%async_computation.11 | async-start | bytes 851968 | tf_op jit(solution)/shard_map/slice | solution.py:63
  93.2 4.5 %copy-start.38 = (f32[256,16]{0,1:T(8,128)S(1)}, f32[256,16]{0,1:T(8,128)}, u32[]{:S(2)}) copy-start(f32[256,16]{0,1:T(8,128)} %get-tuple-element.84) | copy-start | bytes 49156
  93.2 4.5 %copy-start.39 = (f32[256,16]{0,1:T(8,128)S(1)}, f32[256,16]{0,1:T(8,128)}, u32[]{:S(2)}) copy-start(f32[256,16]{0,1:T(8,128)} %get-tuple-element.85) | copy-start | bytes 49156
  98.8 3.3 %slice-start.4 = ((f32[512,256]{0,1:T(8,128)}), f32[512,192]{0,1:T(8,128)S(1)}, s32[]{:S(2)}) async-start(f32[512,256]{0,1:T(8,128)} %copy-done.1), calls=%async_computation.10 | async-start | bytes 786432 | tf_op jit(solution)/shard_map/slice | solution.py:63
  104.1 3.9 %slice-start.6 = ((f32[512,256]{0,1:T(8,128)}), f32[512,224]{0,1:T(8,128)S(1)}, s32[]{:S(2)}) async-start(f32[512,256]{0,1:T(8,128)} %copy-done.1), calls=%async_computation.12 | async-start | bytes 917504 | tf_op jit(solution)/shard_map/slice | solution.py:63
  104.1 3.9 %copy-start.23 = (f32[512,32]{0,1:T(8,128)S(1)}, f32[512,32]{0,1:T(8,128)}, u32[]{:S(2)}) copy-start(f32[512,32]{0,1:T(8,128)} %copy-done.22) | copy-start | bytes 196612
  104.1 3.9 %copy-start.36 = (f32[256,16]{0,1:T(8,128)S(1)}, f32[256,16]{0,1:T(8,128)}, u32[]{:S(2)}) copy-start(f32[256,16]{0,1:T(8,128)} %get-tuple-element.86) | copy-start | bytes 49156
  104.1 3.9 %copy-start.37 = (f32[256,16]{0,1:T(8,128)S(1)}, f32[256,16]{0,1:T(8,128)}, u32[]{:S(2)}) copy-start(f32[256,16]{0,1:T(8,128)} %get-tuple-element.87) | copy-start | bytes 49156
  109.0 3.3 %slice-start.3 = ((f32[512,256]{0,1:T(8,128)}), f32[512,176]{0,1:T(8,128)S(1)}, s32[]{:S(2)}) async-start(f32[512,256]{0,1:T(8,128)} %copy-done.1), calls=%async_computation.9 | async-start | bytes 720896 | tf_op jit(solution)/shard_map/slice | solution.py:63
  114.4 3.3 %slice-start = ((f32[512,256]{0,1:T(8,128)}), f32[512,128]{0,1:T(8,128)S(1)}, s32[]{:S(2)}) async-start(f32[512,256]{0,1:T(8,128)} %copy-done.1), calls=%async_computation.6 | async-start | bytes 524288 | tf_op jit(solution)/shard_map/slice | solution.py:63
  114.4 3.3 %copy-start.26 = (f32[512,16]{0,1:T(8,128)S(1)}, f32[512,16]{0,1:T(8,128)}, u32[]{:S(2)}) copy-start(f32[512,16]{0,1:T(8,128)} %copy-done.25) | copy-start | bytes 98308
  114.4 3.3 %copy-start.33 = (f32[256,16]{0,1:T(8,128)S(1)}, f32[256,16]{0,1:T(8,128)}, u32[]{:S(2)}) copy-start(f32[256,16]{0,1:T(8,128)} %get-tuple-element.60) | copy-start | bytes 49156
  114.4 3.3 %copy-start.34 = (f32[256,16]{0,1:T(8,128)S(1)}, f32[256,16]{0,1:T(8,128)}, u32[]{:S(2)}) copy-start(f32[256,16]{0,1:T(8,128)} %get-tuple-element.61) | copy-start | bytes 49156
  117.7 4.5 %slice-start.1 = ((f32[512,256]{0,1:T(8,128)}), f32[512,144]{0,1:T(8,128)S(1)}, s32[]{:S(2)}) async-start(f32[512,256]{0,1:T(8,128)} %copy-done.1), calls=%async_computation.7 | async-start | bytes 589824 | tf_op jit(solution)/shard_map/slice | solution.py:63
  117.7 4.5 %copy-start.7 = (f32[512,112]{0,1:T(8,128)S(1)}, f32[512,112]{0,1:T(8,128)}, u32[]{:S(2)}) copy-start(f32[512,112]{0,1:T(8,128)} %copy-done.6) | copy-start | bytes 688132
  117.7 4.5 %copy-start.31 = (f32[256,16]{0,1:T(8,128)S(1)}, f32[256,16]{0,1:T(8,128)}, u32[]{:S(2)}) copy-start(f32[256,16]{0,1:T(8,128)} %get-tuple-element.76) | copy-start | bytes 49156
  117.7 4.5 %copy-start.32 = (f32[256,16]{0,1:T(8,128)S(1)}, f32[256,16]{0,1:T(8,128)}, u32[]{:S(2)}) copy-start(f32[256,16]{0,1:T(8,128)} %get-tuple-element.77) | copy-start | bytes 49156
  123.2 3.3 %slice-start.2 = ((f32[512,256]{0,1:T(8,128)}), f32[512,160]{0,1:T(8,128)S(1)}, s32[]{:S(2)}) async-start(f32[512,256]{0,1:T(8,128)} %copy-done.1), calls=%async_computation.8 | async-start | bytes 655360 | tf_op jit(solution)/shard_map/slice | solution.py:63
  123.2 3.3 %copy-start.30 = (f32[256,16]{0,1:T(8,128)S(1)}, f32[256,16]{0,1:T(8,128)}, u32[]{:S(2)}) copy-start(f32[256,16]{0,1:T(8,128)} %get-tuple-element.78) | copy-start | bytes 49156
  123.2 3.3 %copy-start.35 = (f32[256,16]{0,1:T(8,128)S(1)}, f32[256,16]{0,1:T(8,128)}, u32[]{:S(2)}) copy-start(f32[256,16]{0,1:T(8,128)} %get-tuple-element.79) | copy-start | bytes 49156
  128.5 4.5 %copy-start.29 = (f32[512,16]{0,1:T(8,128)S(1)}, f32[512,16]{0,1:T(8,128)}, u32[]{:S(2)}) copy-start(f32[512,16]{0,1:T(8,128)} %reduce_sum.145) | copy-start | bytes 98308
  128.5 19.4 %copy-start.28 = (f32[512,16]{0,1:T(8,128)S(1)}, f32[512,16]{0,1:T(8,128)}, u32[]{:S(2)}) copy-start(f32[512,16]{0,1:T(8,128)} %reduce_sum.157) | copy-start | bytes 98308
  128.5 21.4 %copy-start.27 = (f32[512,16]{0,1:T(8,128)S(1)}, f32[512,16]{0,1:T(8,128)}, u32[]{:S(2)}) copy-start(f32[512,16]{0,1:T(8,128)} %reduce_sum.159) | copy-start | bytes 98308
  128.5 22.0 %copy-start.4 = (f32[512,512]{0,1:T(8,128)S(1)}, f32[512,512]{0,1:T(8,128)}, u32[]{:S(2)}) copy-start(f32[512,512]{0,1:T(8,128)} %maximum_bitcast_fusion) | copy-start | bytes 3145732
  129.6 22.9 %copy-start.13 = (f32[256,256]{0,1:T(8,128)S(1)}, f32[256,256]{0,1:T(8,128)}, u32[]{:S(2)}) copy-start(f32[256,256]{0,1:T(8,128)} %get-tuple-element.148) | copy-start | bytes 786436
  133.0 19.5 %copy-start.14 = (f32[256,256]{0,1:T(8,128)S(1)}, f32[256,256]{0,1:T(8,128)}, u32[]{:S(2)}) copy-start(f32[256,256]{0,1:T(8,128)} %get-tuple-element.149) | copy-start | bytes 786436
  133.0 19.5 %copy-start.15 = (f32[256,256]{0,1:T(8,128)S(1)}, f32[256,256]{0,1:T(8,128)}, u32[]{:S(2)}) copy-start(f32[256,256]{0,1:T(8,128)} %get-tuple-element.158) | copy-start | bytes 786436
  133.0 19.5 %copy-start.16 = (f32[256,256]{0,1:T(8,128)S(1)}, f32[256,256]{0,1:T(8,128)}, u32[]{:S(2)}) copy-start(f32[256,256]{0,1:T(8,128)} %get-tuple-element.159) | copy-start | bytes 786436
  133.0 19.5 %copy-start.17 = (f32[256,256]{0,1:T(8,128)S(1)}, f32[256,256]{0,1:T(8,128)}, u32[]{:S(2)}) copy-start(f32[256,256]{0,1:T(8,128)} %get-tuple-element.160) | copy-start | bytes 786436
  133.0 19.5 %copy-start.18 = (f32[256,256]{0,1:T(8,128)S(1)}, f32[256,256]{0,1:T(8,128)}, u32[]{:S(2)}) copy-start(f32[256,256]{0,1:T(8,128)} %get-tuple-element.161) | copy-start | bytes 786436
  133.0 19.5 %copy-start.19 = (f32[256,256]{0,1:T(8,128)S(1)}, f32[256,256]{0,1:T(8,128)}, u32[]{:S(2)}) copy-start(f32[256,256]{0,1:T(8,128)} %get-tuple-element.162) | copy-start | bytes 786436
  133.1 19.5 %copy-start.20 = (f32[256,256]{0,1:T(8,128)S(1)}, f32[256,256]{0,1:T(8,128)}, u32[]{:S(2)}) copy-start(f32[256,256]{0,1:T(8,128)} %get-tuple-element.163) | copy-start | bytes 786436
  133.1 19.5 %copy-start.21 = (f32[256,256]{0,1:T(8,128)S(1)}, f32[256,256]{0,1:T(8,128)}, u32[]{:S(2)}) copy-start(f32[256,256]{0,1:T(8,128)} %get-tuple-element.36) | copy-start | bytes 786436
  156.8 4.7 %copy-start.24 = (bf16[256,256]{1,0:T(8,128)(2,1)S(1)}, bf16[256,256]{1,0:T(8,128)(2,1)}, u32[]{:S(2)}) copy-start(bf16[256,256]{1,0:T(8,128)(2,1)} %param.6) | copy-start | bytes 393220
  156.8 21.0 %copy-start.11 = (bf16[256,256]{0,1:T(8,128)(2,1)S(1)}, bf16[256,256]{0,1:T(8,128)(2,1)}, u32[]{:S(2)}) copy-start(bf16[256,256]{0,1:T(8,128)(2,1)} %copy-done.10) | copy-start | bytes 393220
  156.8 21.0 %copy-start.42 = (f32[256]{0:T(256)S(1)}, f32[256]{0:T(256)}, u32[]{:S(2)}) copy-start(f32[256]{0:T(256)} %param.9) | copy-start | bytes 3076
  157.9 19.6 %all-to-all-start.2 = ((f32[2,256,256]{1,0,2:T(2,128)}), f32[2,256,256]{1,0,2:T(2,128)S(1)}, u32[]{:S(2)}, u32[]{:S(2)}) async-start(f32[2,256,256]{1,0,2:T(2,128)} %copy.30), calls=%async_computation.2 | async-start | bytes 1048576 | tf_op jit(solution)/shard_map/all_to_all | solution.py:101
  161.5 95.6 %reduce-scatter.2.cloned.1.call-start = ((), (), s32[]{:S(2)}) async-start(), calls=%async_computation.5 | async-start | bytes 2228224 | tf_op jit(solution)/shard_map/reduce_scatter | solution.py:106
  (7 other events, 18.1 us)
Sparse Core Ops, SparseCore 0:
  10.4 54.6 all-gather.1
  180.2 76.7 reduce-scatter.1
where the time goes:
time: 266 us; the launch traced here: 264 us
  waiting for transfers between devices  130 us (49%)
  other arithmetic  54.5 us (20%)
  local copies, waits for them, and re-layouts  28.6 us (11%)
  starting transfers between devices  19.3 us (7%)
  matrix products  17.2 us (6%)
  between operations  14.7 us (6%)
    reduce_scatter x1, waiting for transfers between devices, body(): lax.psum_scatter(partial_out.astype(jnp.bfloat16), 'ch', scatter_dimensio...  76.1 us
    all_gather x1, waiting for transfers between devices, body(): lax.all_gather(cotangent, 'ch', axis=1, tiled=True)  29.8 us
    unnamed x106, local copies, waits for them, and re-layouts  22.3 us
    reduce_sum x16, other arithmetic, body(): lag_terms.append(term.reshape(term.shape[0], ctx_count, width).sum(axis=1))  20.4 us
    sub x11, other arithmetic, spec_product(): real_part = first_real * second_real - others * first_imag * second_imag  18 us
    all_to_all x1, waiting for transfers between devices, body(): lax.all_to_all(jnp.stack([convolved_t, filter_grad_t]), 'ctx', 2, 2, tile...  15.8 us
    all_to_all x1, starting transfers between devices, body(): pair_t = lax.all_to_all(pair, 'ctx', 2, 2, tiled=True)  8.57 us
    concatenate x9, other arithmetic, conj_product(): return jnp.concatenate([real_part, imag_part], axis=-2)  8.04 us
  transfers between devices with their start and end apart: 5, of which 5 were waited for; matrix products, arithmetic and copies ran while one was open for 9% of the time, Pallas kernels for 0%

commit v1 on v0

--- a/solution.py
+++ b/solution.py
@@ -81,7 +81,10 @@
     )
     gate_wide = gating.astype(jnp.float32)
     grad_mixed = upstream * gate_wide
-    grad_t = lax.all_to_all(grad_mixed, "ctx", 1, 1, tiled=True)
+    grad_t = jnp.concatenate(
+        lax.all_to_all(jnp.stack(jnp.split(grad_mixed, lax.axis_size("ctx"), axis=1)), "ctx", 0, 0),
+        axis=1,
+    )
     low_spec = transform(first_half, signal_t)
     high_spec = transform(second_half, signal_t)
     seg_spec = high_spec + shift_blocks(low_spec, 1, width)

time: 266 us -> 275 us (1.034)
  local copies, waits for them, and re-layouts: 28.6 us -> 38.3 us
    unnamed x106 -> x121, local copies, waits for them, and re-layouts: 22.3 us -> 31.4 us
  transfers between devices with their start and end apart: 5 -> 5, of which waited for: 5 -> 5; matrix products, arithmetic and copies ran while one was open for 9% -> 8% of each run, Pallas kernels for 0% -> 0%
where the time goes in v1:
time: 275 us; the launch traced here: 273 us
  waiting for transfers between devices  129 us (47%)
  other arithmetic  54.5 us (20%)
  local copies, waits for them, and re-layouts  38.3 us (14%)
  starting transfers between devices  19.3 us (7%)
  matrix products  16.5 us (6%)
  between operations  14.7 us (5%)
    reduce_scatter x1, waiting for transfers between devices, body(): lax.psum_scatter(partial_out.astype(jnp.bfloat16), 'ch', scatter_dimensio...  75.9 us
    unnamed x121, local copies, waits for them, and re-layouts  31.4 us
    all_gather x1, waiting for transfers between devices, body(): lax.all_gather(cotangent, 'ch', axis=1, tiled=True)  29.8 us
    reduce_sum x16, other arithmetic, body(): lag_terms.append(term.reshape(term.shape[0], ctx_count, width).sum(axis=1))  20.4 us
    sub x11, other arithmetic, spec_product(): real_part = first_real * second_real - others * first_imag * second_imag  18 us
    all_to_all x1, waiting for transfers between devices, body(): lax.all_to_all(jnp.stack([convolved_t, filter_grad_t]), 'ctx', 2, 2, tile...  15.8 us
    all_to_all x1, starting transfers between devices, body(): pair_t = lax.all_to_all(pair, 'ctx', 2, 2, tiled=True)  8.57 us
    concatenate x9, other arithmetic, conj_product(): return jnp.concatenate([real_part, imag_part], axis=-2)  8.04 us
  transfers between devices with their start and end apart: 5, of which 5 were waited for; matrix products, arithmetic and copies ran while one was open for 8% of the time, Pallas kernels for 0%

profile of v1, /device:TPU:2, one launch (start us, length us, event | category | flops | bytes accessed | tf_op | source)
XLA Modules:
  0.0 272.7 jit_solution(9645363618873182372)
XLA Ops:
  9.8 8.6 %all-to-all-start = ((bf16[2,256,256]{1,0,2:T(2,128)(2,1)}), bf16[2,256,256]{1,0,2:T(2,128)(2,1)S(1)}, u32[]{:S(2)}, u32[]{:S(2)}) async-start(bf16[2,256,256]{1,0,2:T(2,128)(2,1)} %copy.25), calls=%async_computation | async-start | bytes 524288 | tf_op jit(solution)/shard_map/all_to_all | solution.py:74
  19.4 1.9 fusion.170
  21.3 2.0 multiply_multiply_fusion
  23.3 2.0 select_multiply_fusion
  26.5 3.0 %all-to-all-done = bf16[2,256,256]{1,0,2:T(2,128)(2,1)S(1)} async-done(((bf16[2,256,256]{1,0,2:T(2,128)(2,1)}), bf16[2,256,256]{1,0,2:T(2,128)(2,1)S(1)}, u32[]{:S(2)}, u32[]{:S(2)}) %all-to-all-start) | async-done | bytes 262176 | tf_op jit(solution)/shard_map/all_to_all | solution.py:74
  29.5 1.2 fusion.195
  32.8 1.3 fusion.173
  34.1 1.3 fusion.175
  35.3 29.8 %all-gather.2.cloned.1.call-done = bf16[256,4096]{1,0:T(8,128)(2,1)} async-done(((bf16[256,256]{1,0:T(8,128)(2,1)}), bf16[256,4096]{1,0:T(8,128)(2,1)}) %all-gather.2.cloned.1.call-update) | async-done | bytes 2097168 | tf_op jit(solution)/shard_map/all_gather | solution.py:77
  65.1 2.3 convolution_multiply_fusion
  77.1 7.1 %all-to-all-start.1 = ((f32[16,256,16]{1,2,0:T(8,128)}), f32[16,256,16]{1,2,0:T(8,128)S(1)}, u32[]{:S(2)}, u32[]{:S(2)}) async-start(f32[16,256,16]{1,2,0:T(8,128)} %constant_dynamic-update-slice_fusion), calls=%async_computation.1 | async-start | bytes 524288 | tf_op jit(solution)/shard_map/all_to_all | solution.py:85
  84.3 1.6 convolution_add_fusion
  89.2 1.3 fusion.128
  91.3 4.2 %all-to-all-done.1 = f32[16,256,16]{1,2,0:T(8,128)S(1)} async-done(((f32[16,256,16]{1,2,0:T(8,128)}), f32[16,256,16]{1,2,0:T(8,128)S(1)}, u32[]{:S(2)}, u32[]{:S(2)}) %all-to-all-start.1) | async-done | bytes 262176 | tf_op jit(solution)/shard_map/all_to_all | solution.py:85
  95.4 1.7 fusion.171
  97.1 1.7 fusion.72
  99.6 2.7 fusion.76
  103.4 1.7 reduce_sum.145
  105.1 1.7 reduce_sum.159
  108.7 1.7 reduce_sum.147
  111.0 2.0 fusion.88
  114.2 1.7 reduce_sum.148
  119.0 1.7 reduce_sum.146
  121.3 2.1 fusion.92
  124.4 1.7 reduce_sum.149
  126.7 1.9 fusion.132
  129.5 1.7 reduce_sum.152
  133.1 1.7 reduce_sum.151
  135.5 2.1 fusion.96
  138.6 1.7 reduce_sum.150
  140.4 1.7 reduce_sum.154
  142.7 1.4 constant_dynamic-update-slice_fusion.29
  144.1 1.4 constant_dynamic-update-slice_fusion.28
  145.4 1.4 constant_dynamic-update-slice_fusion.27
  146.8 1.4 constant_dynamic-update-slice_fusion.26
  148.1 1.4 constant_dynamic-update-slice_fusion.25
  149.5 1.4 constant_dynamic-update-slice_fusion.24
  150.9 1.4 constant_dynamic-update-slice_fusion.23
  152.2 1.4 constant_dynamic-update-slice_fusion.22
  153.6 1.4 constant_dynamic-update-slice_fusion.21
  155.0 1.4 constant_dynamic-update-slice_fusion.20
  157.5 1.4 constant_dynamic-update-slice_fusion.17
  159.5 2.0 convolution_bitcast_fusion
  161.6 4.2 %convolution_bitcast_fusion.1 = f32[1,256,256]{2,1,0:T(8,128)S(1)} fusion(f32[512,512]{0,1:T(8,128)S(1)} %copy-done.4, f32[256,256]{0,1:T(8,128)} %get-tuple-element.37, f32[256,256]{0,1:T(8,128)S(1)} %copy-done.21, f32[256,256]{0,1:T(8,128)} %get-tuple-element.57, f32[256,256]{0,1:T(8,128)} %get-tuple-element.56, f32[256,256]{0,1:T(8,128)} %get-tuple-element.97, ...), kind=kOutput, calls=%fused_computation.3 | convolution fusion | flops 406716416 | bytes 9175040 | tf_op jit(solution)/shard_map/dot_general | solution.py:102
  166.9 3.6 %all-to-all-start.2 = ((f32[2,256,256]{1,0,2:T(2,128)}), f32[2,256,256]{1,0,2:T(2,128)S(1)}, u32[]{:S(2)}, u32[]{:S(2)}) async-start(f32[2,256,256]{1,0,2:T(2,128)} %copy.30), calls=%async_computation.2 | async-start | bytes 1048576 | tf_op jit(solution)/shard_map/all_to_all | solution.py:104
  170.6 15.8 %all-to-all-done.2 = f32[2,256,256]{1,0,2:T(2,128)S(1)} async-done(((f32[2,256,256]{1,0,2:T(2,128)}), f32[2,256,256]{1,0,2:T(2,128)S(1)}, u32[]{:S(2)}, u32[]{:S(2)}) %all-to-all-start.2) | async-done | bytes 524320 | tf_op jit(solution)/shard_map/all_to_all | solution.py:104
  186.9 2.2 convolution_convert_fusion
  189.9 75.9 %reduce-scatter.2.cloned.1.call-done = bf16[256,256]{1,0:T(8,128)(2,1)} async-done(((bf16[256,4096]{1,0:T(8,128)(2,1)}), bf16[256,256]{1,0:T(8,128)(2,1)}) %reduce-scatter.2.cloned.1.call-update) | async-done | bytes 131088 | tf_op jit(solution)/shard_map/reduce_scatter | solution.py:109
  (170 shorter events, 40.9 us)
Async XLA Ops:
  7.2 57.9 %copy-start = (bf16[256,4096]{1,0:T(8,128)(2,1)S(1)}, bf16[256,4096]{1,0:T(8,128)(2,1)}, u32[]{:S(2)}) copy-start(bf16[256,4096]{1,0:T(8,128)(2,1)} %param.10) | copy-start | bytes 6291460
  7.2 57.9 %all-gather.2.cloned.1.call-start = ((), (), s32[]{:S(2)}) async-start(), calls=%async_computation.4 | async-start | bytes 2228224 | tf_op jit(solution)/shard_map/all_gather | solution.py:77
  9.8 19.7 %all-to-all-start = ((bf16[2,256,256]{1,0,2:T(2,128)(2,1)}), bf16[2,256,256]{1,0,2:T(2,128)(2,1)S(1)}, u32[]{:S(2)}, u32[]{:S(2)}) async-start(bf16[2,256,256]{1,0,2:T(2,128)(2,1)} %copy.25), calls=%async_computation | async-start | bytes 524288 | tf_op jit(solution)/shard_map/all_to_all | solution.py:74
  19.4 45.7 %copy-start.10 = (bf16[256,256]{0,1:T(8,128)(2,1)}, bf16[256,256]{0,1:T(8,128)(2,1)S(1)}, u32[]{:S(2)}) copy-start(bf16[256,256]{0,1:T(8,128)(2,1)S(1)} %copy.24) | copy-start | bytes 393220
  21.3 62.9 %copy-start.2 = (f32[256,512]{1,0:T(8,128)}, f32[256,512]{1,0:T(8,128)S(1)}, u32[]{:S(2)}) copy-start(f32[256,512]{1,0:T(8,128)S(1)} %fusion.170) | copy-start | bytes 1572868
  25.4 8.7 %copy-start.3 = (f32[256,512]{1,0:T(8,128)}, f32[256,512]{1,0:T(8,128)S(1)}, u32[]{:S(2)}) copy-start(f32[256,512]{1,0:T(8,128)S(1)} %get-tuple-element.153) | copy-start | bytes 1572868
  77.1 18.3 %all-to-all-start.1 = ((f32[16,256,16]{1,2,0:T(8,128)}), f32[16,256,16]{1,2,0:T(8,128)S(1)}, u32[]{:S(2)}, u32[]{:S(2)}) async-start(f32[16,256,16]{1,2,0:T(8,128)} %constant_dynamic-update-slice_fusion), calls=%async_computation.1 | async-start | bytes 524288 | tf_op jit(solution)/shard_map/all_to_all | solution.py:85
  85.9 11.2 %copy-start.1 = (f32[512,256]{0,1:T(8,128)}, f32[512,256]{0,1:T(8,128)S(1)}, u32[]{:S(2)}) copy-start(f32[512,256]{0,1:T(8,128)S(1)} %convolution_add_fusion) | copy-start | bytes 1572868
  85.9 13.7 %copy-start.25 = (f32[512,16]{0,1:T(8,128)}, f32[512,16]{0,1:T(8,128)S(1)}, u32[]{:S(2)}) copy-start(f32[512,16]{0,1:T(8,128)S(1)} %slice.604) | copy-start | bytes 98308
  85.9 3.3 %copy-start.22 = (f32[512,32]{0,1:T(8,128)}, f32[512,32]{0,1:T(8,128)S(1)}, u32[]{:S(2)}) copy-start(f32[512,32]{0,1:T(8,128)S(1)} %slice.601) | copy-start | bytes 196612
  102.2 4.5 %slice-start.5 = ((f32[512,256]{0,1:T(8,128)}), f32[512,208]{0,1:T(8,128)S(1)}, s32[]{:S(2)}) async-start(f32[512,256]{0,1:T(8,128)} %copy-done.1), calls=%async_computation.11 | async-start | bytes 851968 | tf_op jit(solution)/shard_map/slice | solution.py:63
  102.2 4.5 %copy-start.38 = (f32[256,16]{0,1:T(8,128)S(1)}, f32[256,16]{0,1:T(8,128)}, u32[]{:S(2)}) copy-start(f32[256,16]{0,1:T(8,128)} %get-tuple-element.84) | copy-start | bytes 49156
  102.3 4.5 %copy-start.39 = (f32[256,16]{0,1:T(8,128)S(1)}, f32[256,16]{0,1:T(8,128)}, u32[]{:S(2)}) copy-start(f32[256,16]{0,1:T(8,128)} %get-tuple-element.85) | copy-start | bytes 49156
  107.8 3.3 %slice-start.4 = ((f32[512,256]{0,1:T(8,128)}), f32[512,192]{0,1:T(8,128)S(1)}, s32[]{:S(2)}) async-start(f32[512,256]{0,1:T(8,128)} %copy-done.1), calls=%async_computation.10 | async-start | bytes 786432 | tf_op jit(solution)/shard_map/slice | solution.py:63
  113.1 3.9 %slice-start.6 = ((f32[512,256]{0,1:T(8,128)}), f32[512,224]{0,1:T(8,128)S(1)}, s32[]{:S(2)}) async-start(f32[512,256]{0,1:T(8,128)} %copy-done.1), calls=%async_computation.12 | async-start | bytes 917504 | tf_op jit(solution)/shard_map/slice | solution.py:63
  113.1 3.9 %copy-start.23 = (f32[512,32]{0,1:T(8,128)S(1)}, f32[512,32]{0,1:T(8,128)}, u32[]{:S(2)}) copy-start(f32[512,32]{0,1:T(8,128)} %copy-done.22) | copy-start | bytes 196612
  113.1 3.9 %copy-start.36 = (f32[256,16]{0,1:T(8,128)S(1)}, f32[256,16]{0,1:T(8,128)}, u32[]{:S(2)}) copy-start(f32[256,16]{0,1:T(8,128)} %get-tuple-element.86) | copy-start | bytes 49156
  113.1 3.9 %copy-start.37 = (f32[256,16]{0,1:T(8,128)S(1)}, f32[256,16]{0,1:T(8,128)}, u32[]{:S(2)}) copy-start(f32[256,16]{0,1:T(8,128)} %get-tuple-element.87) | copy-start | bytes 49156
  118.0 3.3 %slice-start.3 = ((f32[512,256]{0,1:T(8,128)}), f32[512,176]{0,1:T(8,128)S(1)}, s32[]{:S(2)}) async-start(f32[512,256]{0,1:T(8,128)} %copy-done.1), calls=%async_computation.9 | async-start | bytes 720896 | tf_op jit(solution)/shard_map/slice | solution.py:63
  123.4 3.3 %slice-start = ((f32[512,256]{0,1:T(8,128)}), f32[512,128]{0,1:T(8,128)S(1)}, s32[]{:S(2)}) async-start(f32[512,256]{0,1:T(8,128)} %copy-done.1), calls=%async_computation.6 | async-start | bytes 524288 | tf_op jit(solution)/shard_map/slice | solution.py:63
  123.4 3.3 %copy-start.26 = (f32[512,16]{0,1:T(8,128)S(1)}, f32[512,16]{0,1:T(8,128)}, u32[]{:S(2)}) copy-start(f32[512,16]{0,1:T(8,128)} %copy-done.25) | copy-start | bytes 98308
  123.4 3.3 %copy-start.33 = (f32[256,16]{0,1:T(8,128)S(1)}, f32[256,16]{0,1:T(8,128)}, u32[]{:S(2)}) copy-start(f32[256,16]{0,1:T(8,128)} %get-tuple-element.60) | copy-start | bytes 49156
  123.4 3.3 %copy-start.34 = (f32[256,16]{0,1:T(8,128)S(1)}, f32[256,16]{0,1:T(8,128)}, u32[]{:S(2)}) copy-start(f32[256,16]{0,1:T(8,128)} %get-tuple-element.61) | copy-start | bytes 49156
  126.7 4.5 %slice-start.1 = ((f32[512,256]{0,1:T(8,128)}), f32[512,144]{0,1:T(8,128)S(1)}, s32[]{:S(2)}) async-start(f32[512,256]{0,1:T(8,128)} %copy-done.1), calls=%async_computation.7 | async-start | bytes 589824 | tf_op jit(solution)/shard_map/slice | solution.py:63
  126.7 4.5 %copy-start.7 = (f32[512,112]{0,1:T(8,128)S(1)}, f32[512,112]{0,1:T(8,128)}, u32[]{:S(2)}) copy-start(f32[512,112]{0,1:T(8,128)} %copy-done.6) | copy-start | bytes 688132
  126.7 4.5 %copy-start.31 = (f32[256,16]{0,1:T(8,128)S(1)}, f32[256,16]{0,1:T(8,128)}, u32[]{:S(2)}) copy-start(f32[256,16]{0,1:T(8,128)} %get-tuple-element.76) | copy-start | bytes 49156
  126.7 4.5 %copy-start.32 = (f32[256,16]{0,1:T(8,128)S(1)}, f32[256,16]{0,1:T(8,128)}, u32[]{:S(2)}) copy-start(f32[256,16]{0,1:T(8,128)} %get-tuple-element.77) | copy-start | bytes 49156
  132.2 3.3 %slice-start.2 = ((f32[512,256]{0,1:T(8,128)}), f32[512,160]{0,1:T(8,128)S(1)}, s32[]{:S(2)}) async-start(f32[512,256]{0,1:T(8,128)} %copy-done.1), calls=%async_computation.8 | async-start | bytes 655360 | tf_op jit(solution)/shard_map/slice | solution.py:63
  132.2 3.3 %copy-start.30 = (f32[256,16]{0,1:T(8,128)S(1)}, f32[256,16]{0,1:T(8,128)}, u32[]{:S(2)}) copy-start(f32[256,16]{0,1:T(8,128)} %get-tuple-element.78) | copy-start | bytes 49156
  132.2 3.3 %copy-start.35 = (f32[256,16]{0,1:T(8,128)S(1)}, f32[256,16]{0,1:T(8,128)}, u32[]{:S(2)}) copy-start(f32[256,16]{0,1:T(8,128)} %get-tuple-element.79) | copy-start | bytes 49156
  137.5 4.5 %copy-start.29 = (f32[512,16]{0,1:T(8,128)S(1)}, f32[512,16]{0,1:T(8,128)}, u32[]{:S(2)}) copy-start(f32[512,16]{0,1:T(8,128)} %reduce_sum.145) | copy-start | bytes 98308
  137.5 19.4 %copy-start.28 = (f32[512,16]{0,1:T(8,128)S(1)}, f32[512,16]{0,1:T(8,128)}, u32[]{:S(2)}) copy-start(f32[512,16]{0,1:T(8,128)} %reduce_sum.157) | copy-start | bytes 98308
  137.5 21.4 %copy-start.27 = (f32[512,16]{0,1:T(8,128)S(1)}, f32[512,16]{0,1:T(8,128)}, u32[]{:S(2)}) copy-start(f32[512,16]{0,1:T(8,128)} %reduce_sum.159) | copy-start | bytes 98308
  137.5 22.0 %copy-start.4 = (f32[512,512]{0,1:T(8,128)S(1)}, f32[512,512]{0,1:T(8,128)}, u32[]{:S(2)}) copy-start(f32[512,512]{0,1:T(8,128)} %maximum_bitcast_fusion) | copy-start | bytes 3145732
  138.6 22.9 %copy-start.13 = (f32[256,256]{0,1:T(8,128)S(1)}, f32[256,256]{0,1:T(8,128)}, u32[]{:S(2)}) copy-start(f32[256,256]{0,1:T(8,128)} %get-tuple-element.148) | copy-start | bytes 786436
  142.0 19.5 %copy-start.14 = (f32[256,256]{0,1:T(8,128)S(1)}, f32[256,256]{0,1:T(8,128)}, u32[]{:S(2)}) copy-start(f32[256,256]{0,1:T(8,128)} %get-tuple-element.149) | copy-start | bytes 786436
  142.0 19.5 %copy-start.15 = (f32[256,256]{0,1:T(8,128)S(1)}, f32[256,256]{0,1:T(8,128)}, u32[]{:S(2)}) copy-start(f32[256,256]{0,1:T(8,128)} %get-tuple-element.158) | copy-start | bytes 786436
  142.0 19.5 %copy-start.16 = (f32[256,256]{0,1:T(8,128)S(1)}, f32[256,256]{0,1:T(8,128)}, u32[]{:S(2)}) copy-start(f32[256,256]{0,1:T(8,128)} %get-tuple-element.159) | copy-start | bytes 786436
  142.0 19.5 %copy-start.17 = (f32[256,256]{0,1:T(8,128)S(1)}, f32[256,256]{0,1:T(8,128)}, u32[]{:S(2)}) copy-start(f32[256,256]{0,1:T(8,128)} %get-tuple-element.160) | copy-start | bytes 786436
  142.1 19.5 %copy-start.18 = (f32[256,256]{0,1:T(8,128)S(1)}, f32[256,256]{0,1:T(8,128)}, u32[]{:S(2)}) copy-start(f32[256,256]{0,1:T(8,128)} %get-tuple-element.161) | copy-start | bytes 786436
  142.1 19.5 %copy-start.19 = (f32[256,256]{0,1:T(8,128)S(1)}, f32[256,256]{0,1:T(8,128)}, u32[]{:S(2)}) copy-start(f32[256,256]{0,1:T(8,128)} %get-tuple-element.162) | copy-start | bytes 786436
  142.1 19.5 %copy-start.20 = (f32[256,256]{0,1:T(8,128)S(1)}, f32[256,256]{0,1:T(8,128)}, u32[]{:S(2)}) copy-start(f32[256,256]{0,1:T(8,128)} %get-tuple-element.163) | copy-start | bytes 786436
  142.1 19.5 %copy-start.21 = (f32[256,256]{0,1:T(8,128)S(1)}, f32[256,256]{0,1:T(8,128)}, u32[]{:S(2)}) copy-start(f32[256,256]{0,1:T(8,128)} %get-tuple-element.36) | copy-start | bytes 786436
  165.8 4.7 %copy-start.24 = (bf16[256,256]{1,0:T(8,128)(2,1)S(1)}, bf16[256,256]{1,0:T(8,128)(2,1)}, u32[]{:S(2)}) copy-start(bf16[256,256]{1,0:T(8,128)(2,1)} %param.6) | copy-start | bytes 393220
  165.8 21.0 %copy-start.11 = (bf16[256,256]{0,1:T(8,128)(2,1)S(1)}, bf16[256,256]{0,1:T(8,128)(2,1)}, u32[]{:S(2)}) copy-start(bf16[256,256]{0,1:T(8,128)(2,1)} %copy-done.10) | copy-start | bytes 393220
  165.9 21.0 %copy-start.42 = (f32[256]{0:T(256)S(1)}, f32[256]{0:T(256)}, u32[]{:S(2)}) copy-start(f32[256]{0:T(256)} %param.9) | copy-start | bytes 3076
  166.9 19.6 %all-to-all-start.2 = ((f32[2,256,256]{1,0,2:T(2,128)}), f32[2,256,256]{1,0,2:T(2,128)S(1)}, u32[]{:S(2)}, u32[]{:S(2)}) async-start(f32[2,256,256]{1,0,2:T(2,128)} %copy.30), calls=%async_computation.2 | async-start | bytes 1048576 | tf_op jit(solution)/shard_map/all_to_all | solution.py:104
  170.5 95.4 %reduce-scatter.2.cloned.1.call-start = ((), (), s32[]{:S(2)}) async-start(), calls=%async_computation.5 | async-start | bytes 2228224 | tf_op jit(solution)/shard_map/reduce_scatter | solution.py:109
  (7 other events, 18.1 us)
Sparse Core Ops, SparseCore 0:
  10.4 54.6 all-gather.1
  189.2 76.5 reduce-scatter.1
